TPU v7x, 32 devices: a whole 2x2x4 slice. The times are simulated.
32 devices in a mesh: tm: 4 (over y, x), series: 8 (over z, core).
Axes of the slice: x: 2, y: 2, z: 4, core: 2. Of those that a mesh axis runs over, the one named last changes fastest.
Arguments:
- codes: int32 [8, 512], P(None, ('tm', 'series')), may hold values from 0 to 916478, as said below
- owner_slot: int32 [8], replicated, may hold values from 0 to 7, each once
- edges: int32 [4096], replicated, may hold values from 0 to 2096640, as said below
- w_in: bfloat16 [128, 2304], replicated, may hold values from -0.09375 to 0.09375
- w_dt: bfloat16 [128, 32], replicated, may hold values from -0.5 to 0.5
- dt_bias: float32 [32], replicated, may hold values from -1 to 1
- decay_rate: float32 [32], replicated, may hold values from 1e-05 to 0.1
- grad_out: bfloat16 [8, 512, 2048], P('series', 'tm'), may hold values from -6 to 6
Outputs:
- ssd_output: bfloat16 [8, 512, 2048], P('series', 'tm')
- grad_in: float32 [128, 2304], replicated
Inputs may be any that keep to these rules, and one draw needn't show every extreme that they name: `codes`: each row is one series in the order of ingestion slots. edges[0] is 0 and edges rise strictly.
All inputs are finite; a program needn't handle non-finite values.
Results may differ from a plain program's by a relative error of at most 0.0062.
The roundings to bfloat16 on the way count: a program that leaves them out, or rounds other values in their place, can miss the bound.
Values sent between devices are 32-bit elements; how exact they have to be, the bound alone decides.
No kernel may reach another device: no remote copies, remote signals or barrier semaphores. Data moves between devices by JAX's collectives and lax.ppermute only.
A program may use at most 128 MiB of HBM per device.

v0:
```python
import math
import jax
import jax.numpy as jnp
from jax import lax
from jax.sharding import PartitionSpec as P

code_ceiling = 2097152.0


def decay_matrix(cum_decay):
    row_count = cum_decay.shape[0]
    causal = jnp.arange(row_count)[:, None] >= jnp.arange(row_count)[None, :]
    log_span = cum_decay.T[:, :, None] - cum_decay.T[:, None, :]
    return jnp.where(causal[None], jnp.exp(jnp.where(causal[None], log_span, -60.0)), 0.0)


def on_device(codes, owner_slot, edges, w_in, w_dt, dt_bias, decay_rate, grad_out):
    fl = jnp.float32
    half = jnp.bfloat16
    tok_rows = grad_out.shape[1]
    head_count = dt_bias.shape[0]
    inner_width = grad_out.shape[2]
    head_dim = inner_width // head_count
    state_dim = (w_in.shape[1] - inner_width) // 2
    n_blocks = lax.axis_size("tm")
    seq_len = tok_rows * n_blocks
    series_count = lax.axis_size("series")
    my_block = lax.axis_index("tm")
    my_series = lax.axis_index("series")
    all_codes = lax.all_gather(codes, ("tm", "series"), axis=1, tiled=True)
    row = lax.dynamic_index_in_dim(all_codes, owner_slot[my_series], axis=0, keepdims=False)
    reading = row.astype(fl)
    edge_float = edges.astype(fl)
    upper_edge = jnp.concatenate([edge_float[1:], jnp.full((1,), code_ceiling, fl)])
    onehot = (
        (edge_float[None, :] <= reading[:, None]) & (upper_edge[None, :] > reading[:, None])
    ).astype(fl)
    counts = jnp.sum(onehot, axis=0)
    before = jnp.cumsum(counts) - counts
    bin_table = jnp.stack([before, counts, edge_float, upper_edge - edge_float], axis=1)
    picked = jnp.dot(onehot, bin_table, precision=lax.Precision.HIGHEST)
    within_bin = (reading - picked[:, 2]) / picked[:, 3]
    quantile = (picked[:, 0] + picked[:, 1] * within_bin) / seq_len
    frequency = (jnp.arange(w_in.shape[0], dtype=fl) + 0.5) * math.pi
    features_all = jnp.cos(quantile[:, None] * frequency).astype(half)
    projected_all = jnp.dot(features_all, w_in, preferred_element_type=fl).astype(half)
    projected_all = projected_all.reshape(n_blocks, tok_rows, -1)
    x_all = projected_all[:, :, :inner_width].reshape(n_blocks, tok_rows, head_count, head_dim)
    b_all = projected_all[:, :, inner_width : inner_width + state_dim]
    c_all = projected_all[:, :, inner_width + state_dim :]
    step_all = jax.nn.softplus(
        dt_bias + jnp.dot(features_all, w_dt, preferred_element_type=fl)
    ).reshape(n_blocks, tok_rows, head_count)
    cum_all = jnp.cumsum(-step_all * decay_rate, axis=1)
    gate_all = jnp.exp(cum_all[:, -1])
    tail_all = jnp.exp(cum_all[:, -1:, :] - cum_all) * step_all
    xw_all = (x_all * tail_all[..., None]).astype(half)
    state_local_all = jnp.einsum("bthp,btn->bhpn", xw_all, b_all, preferred_element_type=fl)
    state_in = jnp.zeros((head_count, head_dim, state_dim), fl)
    for k in range(n_blocks - 1):
        new = gate_all[k][:, None, None] * state_in + state_local_all[k]
        state_in = jnp.where(k < my_block, new, state_in)

    def mine(a):
        return lax.dynamic_index_in_dim(a, my_block, axis=0, keepdims=False)

    features = mine(features_all.reshape(n_blocks, tok_rows, -1))
    x_heads = mine(x_all)
    b_proj = mine(b_all)
    c_proj = mine(c_all)
    step_size = mine(step_all)
    cum_decay = mine(cum_all)
    tail_factor = mine(tail_all)
    x_weighted = mine(xw_all)
    head_factor = jnp.exp(cum_decay)
    grad_heads = grad_out[0].reshape(tok_rows, head_count, head_dim)
    grad_weighted = (grad_heads * head_factor[:, :, None]).astype(half)
    adjoint_local = jnp.einsum("thp,tn->hpn", grad_weighted, c_proj, preferred_element_type=fl)
    adjoint_all = lax.all_gather(adjoint_local, "tm")
    adjoint_in = jnp.zeros((head_count, head_dim, state_dim), fl)
    for k in range(n_blocks - 1, 0, -1):
        new = gate_all[k][:, None, None] * adjoint_in + adjoint_all[k]
        adjoint_in = jnp.where(k > my_block, new, adjoint_in)
    masked = decay_matrix(cum_decay) * step_size.T[:, None, :]
    scores = jnp.dot(c_proj, b_proj.T, preferred_element_type=fl)
    weights = (scores[None] * masked).astype(half)
    state_half = state_in.astype(half)
    adjoint_half = adjoint_in.astype(half)
    output = jnp.einsum("hts,shp->thp", weights, x_heads, preferred_element_type=fl)
    output = (
        output
        + jnp.einsum("tn,hpn->thp", c_proj, state_half, preferred_element_type=fl)
        * head_factor[:, :, None]
    )
    ssd_output = output.reshape(1, tok_rows, inner_width).astype(half)
    grad_x = jnp.einsum("hts,thp->shp", weights, grad_heads, preferred_element_type=fl)
    grad_x = (
        grad_x
        + jnp.einsum("sn,hpn->shp", b_proj, adjoint_half, preferred_element_type=fl)
        * tail_factor[:, :, None]
    )
    pair_scores = jnp.einsum("thp,shp->hts", grad_heads, x_heads, preferred_element_type=fl)
    pair_mixed = jnp.sum(pair_scores * masked, axis=0).astype(half)
    grad_b = jnp.dot(pair_mixed.T, c_proj, preferred_element_type=fl)
    grad_b = grad_b + jnp.einsum("shp,hpn->sn", x_weighted, adjoint_half, preferred_element_type=fl)
    grad_c = jnp.dot(pair_mixed, b_proj, preferred_element_type=fl)
    grad_c = grad_c + jnp.einsum(
        "thp,hpn->tn", grad_weighted, state_half, preferred_element_type=fl
    )
    grad_rows = jnp.concatenate(
        [
            grad_x.reshape(tok_rows, inner_width).astype(half),
            grad_b.astype(half),
            grad_c.astype(half),
        ],
        axis=1,
    )
    local_grad = jnp.einsum("tf,tw->fw", features, grad_rows, preferred_element_type=fl)
    share_grad = lax.psum_scatter(local_grad, "series", scatter_dimension=1, tiled=True)
    share_grad = lax.psum(share_grad, "tm")
    total_grad = lax.all_gather(share_grad, "series", axis=1, tiled=True)
    grad_in = total_grad / math.sqrt(series_count * seq_len)
    return (ssd_output, grad_in)


def solution(mesh):
    return jax.shard_map(
        on_device,
        mesh=mesh,
        in_specs=(P(None, ("tm", "series")), P(), P(), P(), P(), P(), P(), P("series", "tm", None)),
        out_specs=(P("series", "tm", None), P()),
        check_vma=False,
    )
```

profile of v0, /device:TPU:0, one launch (start us, length us, event | category | flops | bytes accessed | tf_op | source)
XLA Modules:
  0.0 243.4 jit_solution(498775291195324287)
XLA Ops:
  7.2 1.3 dynamic_slice.34
  9.8 44.0 %all-gather.1 = s32[32,16,8]{1,2,0:T(8,128)S(1)} all-gather(s32[1,16,8]{1,2,0:T(8,128)} %bitcast.172), channel_id=1, replica_groups=mesh['tm'=4,'series'=8] {'tm','series'}, dimensions={0}, use_global_device_ids=true | all-gather | bytes 16896 | tf_op jit(solution)/shard_map/all_gather | solution.py:30
  56.2 1.4 convert_reduce_fusion
  58.3 4.1 %fusion = f32[512,4]{0,1:T(4,128)S(1)} fusion(f32[4096]{0:T(1024)S(1)} %get-tuple-element.13, f32[4096]{0:T(1024)S(1)} %convert_element_type.97, f32[512]{0:T(512)S(1)} %bitcast.168, f32[4096,1]{0,1:T(1,128)S(1)} %bitcast.166, f32[4096,1]{0,1:T(1,128)S(1)} %bitcast.155, f32[4096,1]{0,1:T(1,128)S(1)} %bitcast.154, f32[4096,1]{0,1:T(1,128)S(1)} %sub.42), kind=kOutput, calls=%fused_computation.2 | convolution fusion | flops 107003904 | bytes 108544 | tf_op jit(solution)/shard_map/dot_general | solution.py:41
  62.5 1.6 convolution_convert_fusion
  64.2 1.1 compare_select_fusion
  66.2 1.2 reduce_window_sum.35
  68.9 1.5 copy.57
  71.1 2.0 copy.61
  73.2 1.1 fusion.24
  75.1 2.0 fusion.59
  77.4 1.6 slice.98
  79.6 3.2 %copy.54 = bf16[4,128,2048]{1,2,0:T(8,128)(2,1)S(1)} copy(bf16[4,128,2048]{2,1,0:T(8,128)(2,1)} %slice.98) | data formatting | bytes 4194304 | tf_op jit(solution)/shard_map/slice | solution.py:48
  82.8 1.2 exp.26
  84.0 1.7 exponential_multiply_fusion
  85.7 1.0 copy.60
  88.3 1.2 constant_dynamic-slice_fusion.1
  90.4 1.4 multiply_bitcast_fusion
  91.9 2.4 fusion.4
  96.3 2.3 convolution_bitcast_fusion
  99.3 3.6 %fusion.41 = f32[4,32,64,128]{3,2,1,0:T(8,128)} fusion(bf16[4,128,32,64]{1,3,2,0:T(8,128)(2,1)S(1)} %multiply_convert_fusion, bf16[4,128,2304]{2,1,0:T(8,128)(2,1)} %bitcast.143), kind=kOutput, calls=%fused_computation.67 | convolution fusion | flops 268435456 | bytes 6422528 | tf_op jit(solution)/shard_map/bthp,btn->bhpn/dot_general | solution.py:58
  102.9 23.4 %all-gather.7.cloned.1.call-done = f32[128,64,128]{2,1,0:T(8,128)} async-done(((f32[32,64,128]{2,1,0:T(8,128)}), f32[128,64,128]{2,1,0:T(8,128)}) %all-gather.7.cloned.1.call-update) | async-done | bytes 4194320 | tf_op jit(solution)/shard_map/all_gather | solution.py:79
  126.3 3.6 %fusion.15 = (bf16[1,32,64,128]{3,2,1,0:T(8,128)(2,1)S(1)}, bf16[1,32,64,128]{3,2,1,0:T(8,128)(2,1)S(1)}) fusion(f32[128,64,128]{2,1,0:T(8,128)} %all-gather.7.cloned.1.call-done, f32[32]{0:T(128)S(1)} %copy-done.19, f32[32]{0:T(128)S(1)} %copy-done.21, f32[32]{0:T(128)S(1)} %copy-done.22, pred[]{:T(512)S(6)} %lt.34, pred[]{:T(512)S(6)} %lt.33, pred[]{:T(512)S(6)} %lt.32, ...), kind=kLoop, calls=%fused_computation.30 | loop fusion | flops 4718592 | bytes 7340550 | tf_op jit(solution)/shard_map/convert_element_type | solution.py:88
  130.3 1.1 fusion.8
  131.8 1.6 fusion.25
  133.5 32.8 %reduce-scatter.2.cloned.1.call-done = f32[128,288]{0,1:T(8,128)} async-done(((f32[128,2304]{0,1:T(8,128)}), f32[128,288]{0,1:T(8,128)}) %reduce-scatter.2.cloned.1.call-update) | async-done | bytes 147472 | tf_op jit(solution)/shard_map/reduce_scatter | solution.py:119
  166.3 43.3 %all-reduce.2.cloned.1.call-done = f32[128,288]{0,1:T(8,128)} async-done(((f32[128,288]{0,1:T(8,128)}), f32[128,288]{0,1:T(8,128)}) %all-reduce.2.cloned.1.call-update) | async-done | bytes 147472 | tf_op jit(solution)/shard_map/psum | solution.py:120
  209.7 3.3 %convolution_bitcast_fusion.1 = f32[128,32,64]{0,2,1:T(8,128)S(1)} fusion(f32[32,128]{1,0:T(8,128)S(1)} %bitcast.165, f32[32,128]{1,0:T(8,128)S(1)} %bitcast.159, f32[128,128]{0,1:T(8,128)S(1)} %copy-done.13, pred[128,128]{0,1:T(8,128)(4,1)S(1)} %copy-done.17, bf16[4,128,32,64]{1,3,2,0:T(8,128)(2,1)} %bitcast.145, s32[]{:T(128)S(6)} %select_n.83), kind=kOutput, calls=%fused_computation.17 | convolution fusion | flops 70254592 | bytes 1703940 | tf_op jit(solution)/shard_map/hts,shp->thp/dot_general | solution.py:89
  213.0 1.1 fusion.7
  215.1 19.0 %all-gather.5.cloned.1.call-done = f32[128,2304]{0,1:T(8,128)} async-done(((f32[128,288]{0,1:T(8,128)}), f32[128,2304]{0,1:T(8,128)}) %all-gather.5.cloned.1.call-update) | async-done | bytes 1179664 | tf_op jit(solution)/shard_map/all_gather | solution.py:121
  234.1 1.3 broadcast_multiply_fusion
  235.5 1.4 copy.66
  (98 shorter events, 14.1 us)
Async XLA Ops:
  7.2 55.4 %copy-start = (bf16[128,2304]{1,0:T(8,128)(2,1)S(1)}, bf16[128,2304]{1,0:T(8,128)(2,1)}, u32[]{:S(2)}) copy-start(bf16[128,2304]{1,0:T(8,128)(2,1)} %param.11) | copy-start | bytes 1769476
  7.2 119.1 %all-gather.7.cloned.1.call-start = ((), (), s32[]{:S(2)}) async-start(), calls=%async_computation.4 | async-start | bytes 5242880 | tf_op jit(solution)/shard_map/all_gather | solution.py:79
  9.8 54.3 %copy-start.23 = (f32[128]{0:T(128)}, f32[128]{0:T(128)S(1)}, u32[]{:S(2)}) copy-start(f32[128]{0:T(128)S(1)} %add_multiply_fusion) | copy-start | bytes 1540
  62.4 1.7 copy-start.27
  62.5 1.7 copy-start.28
  62.5 3.0 %copy-start.25 = (f32[32]{0:T(128)S(1)}, f32[32]{0:T(128)}, u32[]{:S(2)}) copy-start(f32[32]{0:T(128)} %param.14) | copy-start | bytes 388
  62.5 2.8 %copy-start.18 = (f32[512,1]{0,1:T(1,128)}, f32[512,1]{0,1:T(1,128)S(1)}, u32[]{:S(2)}) copy-start(f32[512,1]{0,1:T(1,128)S(1)} %fusion.89) | copy-start | bytes 6148
  64.2 13.2 %copy-start.1 = (bf16[512,2304]{1,0:T(8,128)(2,1)}, bf16[512,2304]{1,0:T(8,128)(2,1)S(1)}, u32[]{:S(2)}) copy-start(bf16[512,2304]{1,0:T(8,128)(2,1)S(1)} %convolution_convert_fusion) | copy-start | bytes 7077892
  67.4 11.6 %copy-start.7 = (f32[4,128,32]{2,1,0:T(8,128)}, f32[4,128,32]{2,1,0:T(8,128)S(1)}, u32[]{:S(2)}) copy-start(f32[4,128,32]{2,1,0:T(8,128)S(1)} %reduce_window_sum.35) | copy-start | bytes 196612
  77.1 89.1 %reduce-scatter.2.cloned.1.call-start = ((), (), s32[]{:S(2)}) async-start(), calls=%async_computation.1 | async-start | bytes 1327104 | tf_op jit(solution)/shard_map/reduce_scatter | solution.py:119
  79.6 12.3 %copy-start.6 = (bf16[1,128,2048]{1,2,0:T(8,128)(2,1)S(1)}, bf16[1,128,2048]{1,2,0:T(8,128)(2,1)}, u32[]{:S(2)}) copy-start(bf16[1,128,2048]{1,2,0:T(8,128)(2,1)} %copy.61) | copy-start | bytes 1572868
  82.8 11.5 %copy-start.2 = (bf16[4,128,2048]{1,2,0:T(8,128)(2,1)}, bf16[4,128,2048]{1,2,0:T(8,128)(2,1)S(1)}, u32[]{:S(2)}) copy-start(bf16[4,128,2048]{1,2,0:T(8,128)(2,1)S(1)} %copy.54) | copy-start | bytes 6291460
  89.5 6.7 %copy-start.14 = (f32[1,128,32]{1,0,2:T(1,128)}, f32[1,128,32]{1,0,2:T(1,128)S(1)}, u32[]{:S(2)}) copy-start(f32[1,128,32]{1,0,2:T(1,128)S(1)} %constant_dynamic-slice_fusion.2) | copy-start | bytes 49156
  89.5 6.7 %copy-start.16 = (pred[128,128]{0,1:T(8,128)(4,1)}, pred[128,128]{0,1:T(8,128)(4,1)S(1)}, u32[]{:S(2)}) copy-start(pred[128,128]{0,1:T(8,128)(4,1)S(1)} %iota_compare_fusion) | copy-start | bytes 49156
  90.4 5.8 %copy-start.12 = (f32[128,128]{0,1:T(8,128)}, f32[128,128]{0,1:T(8,128)S(1)}, u32[]{:S(2)}) copy-start(f32[128,128]{0,1:T(8,128)S(1)} %fusion.64) | copy-start | bytes 196612
  91.9 4.4 %copy-start.10 = (f32[1,128,32]{1,2,0:T(8,128)S(1)}, f32[1,128,32]{1,2,0:T(8,128)}, u32[]{:S(2)}) copy-start(f32[1,128,32]{1,2,0:T(8,128)} %copy.57) | copy-start | bytes 49156
  96.3 2.4 copy-start.3
  99.3 27.0 %copy-start.19 = (f32[32]{0:T(128)S(1)}, f32[32]{0:T(128)}, u32[]{:S(2)}) copy-start(f32[32]{0:T(128)} %get-tuple-element.14) | copy-start | bytes 388
  99.3 27.0 %copy-start.20 = (f32[32]{0:T(128)S(1)}, f32[32]{0:T(128)}, u32[]{:S(2)}) copy-start(f32[32]{0:T(128)} %get-tuple-element.15) | copy-start | bytes 388
  99.3 27.0 %copy-start.21 = (f32[32]{0:T(128)S(1)}, f32[32]{0:T(128)}, u32[]{:S(2)}) copy-start(f32[32]{0:T(128)} %get-tuple-element.16) | copy-start | bytes 388
  99.3 27.0 %copy-start.22 = (f32[32]{0:T(128)S(1)}, f32[32]{0:T(128)}, u32[]{:S(2)}) copy-start(f32[32]{0:T(128)} %get-tuple-element.17) | copy-start | bytes 388
  126.3 4.0 %copy-start.8 = (f32[128,32,64]{0,2,1:T(8,128)S(1)}, f32[128,32,64]{0,2,1:T(8,128)}, u32[]{:S(2)}) copy-start(f32[128,32,64]{0,2,1:T(8,128)} %convolution_bitcast_fusion) | copy-start | bytes 3145732
  126.3 4.0 %copy-start.9 = (f32[1,128,32]{1,2,0:T(8,128)S(1)}, f32[1,128,32]{1,2,0:T(8,128)}, u32[]{:S(2)}) copy-start(f32[1,128,32]{1,2,0:T(8,128)} %copy.64) | copy-start | bytes 49156
  129.9 1.5 copy-start.5
  129.9 1.9 copy-start.24
  129.9 1.9 copy-start.26
  131.4 78.3 %copy-start.11 = (f32[1,128,32]{1,2,0:T(8,128)S(1)}, f32[1,128,32]{1,2,0:T(8,128)}, u32[]{:S(2)}) copy-start(f32[1,128,32]{1,2,0:T(8,128)} %copy.57) | copy-start | bytes 49156
  131.4 78.3 %copy-start.13 = (f32[128,128]{0,1:T(8,128)S(1)}, f32[128,128]{0,1:T(8,128)}, u32[]{:S(2)}) copy-start(f32[128,128]{0,1:T(8,128)} %copy-done.12) | copy-start | bytes 196612
  131.4 78.3 %copy-start.15 = (f32[1,128,32]{1,0,2:T(1,128)S(1)}, f32[1,128,32]{1,0,2:T(1,128)}, u32[]{:S(2)}) copy-start(f32[1,128,32]{1,0,2:T(1,128)} %copy-done.14) | copy-start | bytes 49156
  131.4 78.3 %copy-start.17 = (pred[128,128]{0,1:T(8,128)(4,1)S(1)}, pred[128,128]{0,1:T(8,128)(4,1)}, u32[]{:S(2)}) copy-start(pred[128,128]{0,1:T(8,128)(4,1)} %copy-done.16) | copy-start | bytes 49156
  133.4 76.2 %all-reduce.2.cloned.1.call-start = ((), (), s32[]{:S(2)}) async-start(), calls=%async_computation.2 | async-start | bytes 294912 | tf_op jit(solution)/shard_map/psum | solution.py:120
  166.3 67.8 %all-gather.5.cloned.1.call-start = ((), (), s32[]{:S(2)}) async-start(), calls=%async_computation.3 | async-start | bytes 1327104 | tf_op jit(solution)/shard_map/all_gather | solution.py:121
  (1 other events, 0.8 us)
Sparse Core Ops, SparseCore 0:
  77.3 48.9 all-gather.6
  133.6 32.6 reduce-scatter.1
  169.2 40.4 all-reduce.1
  211.3 22.8 all-gather.4
where the time goes:
time: 245 us; the launch traced here: 243 us
  waiting for transfers between devices  119 us (49%)
  blocking collectives  44 us (18%)
  matrix products  27.7 us (11%)
  local copies, waits for them, and re-layouts  21.2 us (9%)
  between operations  16.2 us (7%)
  other arithmetic  15.3 us (6%)
    all_gather x1, blocking collectives, on_device(): all_codes = lax.all_gather(codes, ('tm', 'series'), axis=1, tiled=True)  44 us
    psum x1, waiting for transfers between devices, on_device(): share_grad = lax.psum(share_grad, 'tm')  43.3 us
    reduce_scatter x1, waiting for transfers between devices, on_device(): lax.psum_scatter(local_grad, 'series', scatter_dimension=1, tiled=True)  32.8 us
    all_gather x1, waiting for transfers between devices, on_device(): adjoint_all = lax.all_gather(adjoint_local, 'tm')  23.4 us
    all_gather x1, waiting for transfers between devices, on_device(): total_grad = lax.all_gather(share_grad, 'series', axis=1, tiled=True)  19 us
    unnamed x62, local copies, waits for them, and re-layouts  5.44 us
  transfers between devices with their start and end apart: 4, of which 4 were waited for; matrix products, arithmetic and copies ran while one was open for 13% of the time, Pallas kernels for 0%

commit v1 on v0

--- a/solution.py
+++ b/solution.py
@@ -118,7 +118,21 @@
     local_grad = jnp.einsum("tf,tw->fw", features, grad_rows, preferred_element_type=fl)
     share_grad = lax.psum_scatter(local_grad, "series", scatter_dimension=1, tiled=True)
     share_grad = lax.psum(share_grad, "tm")
-    total_grad = lax.all_gather(share_grad, "series", axis=1, tiled=True)
+    n_shards = lax.axis_size("series")
+    steps_seen = []
+    for i in range(1, n_shards):
+        steps_seen.append((i - 1, i))
+    current_value = steps_seen + [(n_shards - 1, 0)]
+    t_next = share_grad
+    found = [t_next]
+    for _ in range(n_shards - 1):
+        t_next = lax.ppermute(t_next, "series", current_value)
+        found += [t_next]
+    total_grad = jnp.roll(
+        jnp.concatenate([*reversed(found)], 1),
+        shift=(lax.axis_index("series") + 1) * t_next.shape[1],
+        axis=1,
+    )
     grad_in = total_grad / math.sqrt(series_count * seq_len)
     return (ssd_output, grad_in)
 

time: 245 us -> 264 us (1.078)
  waiting for transfers between devices: 119 us -> 138 us
    ppermute x0 -> x7, waiting for transfers between devices: none -> 39.4 us  [on_device(): t_next = lax.ppermute(t_next, 'series', current_value)]
    all_gather x1 -> x0, waiting for transfers between devices: 19 us -> none  [on_device(): total_grad = lax.all_gather(share_grad, 'series', axis=1, tiled=True)]
    unnamed x62 -> x81, local copies, waits for them, and re-layouts: 5.44 us -> 5.65 us
  transfers between devices with their start and end apart: 4 -> 10, of which waited for: 4 -> 10; matrix products, arithmetic and copies ran while one was open for 13% -> 12% of each run, Pallas kernels for 0% -> 0%
where the time goes in v1:
time: 264 us; the launch traced here: 263 us
  waiting for transfers between devices  138 us (52%)
  blocking collectives  44 us (17%)
  matrix products  28.4 us (11%)
  local copies, waits for them, and re-layouts  21.7 us (8%)
  between operations  16.4 us (6%)
  other arithmetic  14.1 us (5%)
    all_gather x1, blocking collectives, on_device(): all_codes = lax.all_gather(codes, ('tm', 'series'), axis=1, tiled=True)  44 us
    psum x1, waiting for transfers between devices, on_device(): share_grad = lax.psum(share_grad, 'tm')  43.2 us
    ppermute x7, waiting for transfers between devices, on_device(): t_next = lax.ppermute(t_next, 'series', current_value)  39.4 us
    reduce_scatter x1, waiting for transfers between devices, on_device(): lax.psum_scatter(local_grad, 'series', scatter_dimension=1, tiled=True)  32.9 us
    all_gather x1, waiting for transfers between devices, on_device(): adjoint_all = lax.all_gather(adjoint_local, 'tm')  22.4 us
    unnamed x81, local copies, waits for them, and re-layouts  5.65 us
  transfers between devices with their start and end apart: 10, of which 10 were waited for; matrix products, arithmetic and copies ran while one was open for 12% of the time, Pallas kernels for 0%

profile of v1, /device:TPU:0, one launch (start us, length us, event | category | flops | bytes accessed | tf_op | source)
XLA Modules:
  0.0 262.8 jit_solution(9324722986071684134)
XLA Ops:
  7.2 1.3 dynamic_slice.38
  9.8 44.0 %all-gather.1 = s32[32,16,8]{1,2,0:T(8,128)S(1)} all-gather(s32[1,16,8]{1,2,0:T(8,128)} %bitcast.172), channel_id=1, replica_groups=mesh['tm'=4,'series'=8] {'tm','series'}, dimensions={0}, use_global_device_ids=true | all-gather | bytes 16896 | tf_op jit(solution)/shard_map/all_gather | solution.py:30
  56.2 1.4 convert_reduce_fusion
  58.3 4.1 %fusion = f32[512,4]{0,1:T(4,128)S(1)} fusion(f32[4096]{0:T(1024)S(1)} %get-tuple-element.13, f32[4096]{0:T(1024)S(1)} %convert_element_type.97, f32[512]{0:T(512)S(1)} %bitcast.168, f32[4096,1]{0,1:T(1,128)S(1)} %bitcast.166, f32[4096,1]{0,1:T(1,128)S(1)} %bitcast.155, f32[4096,1]{0,1:T(1,128)S(1)} %bitcast.154, f32[4096,1]{0,1:T(1,128)S(1)} %sub.46), kind=kOutput, calls=%fused_computation.2 | convolution fusion | flops 107003904 | bytes 108544 | tf_op jit(solution)/shard_map/dot_general | solution.py:41
  62.5 1.6 convolution_convert_fusion
  68.9 1.5 copy.57
  71.1 2.0 copy.61
  75.1 2.0 fusion.59
  77.4 1.6 slice.98
  79.6 3.2 %copy.54 = bf16[4,128,2048]{1,2,0:T(8,128)(2,1)S(1)} copy(bf16[4,128,2048]{2,1,0:T(8,128)(2,1)} %slice.98) | data formatting | bytes 4194304 | tf_op jit(solution)/shard_map/slice | solution.py:48
  82.8 1.4 exp.26
  84.2 1.7 exponential_multiply_fusion
  88.5 1.2 constant_dynamic-slice_fusion.1
  90.7 1.4 multiply_bitcast_fusion
  92.2 2.4 fusion.4
  94.6 1.6 fusion.66
  97.2 2.4 convolution_bitcast_fusion
  100.3 3.6 %fusion.41 = f32[4,32,64,128]{3,2,1,0:T(8,128)} fusion(bf16[4,128,32,64]{1,3,2,0:T(8,128)(2,1)S(1)} %multiply_convert_fusion, bf16[4,128,2304]{2,1,0:T(8,128)(2,1)} %bitcast.143), kind=kOutput, calls=%fused_computation.67 | convolution fusion | flops 268435456 | bytes 6422528 | tf_op jit(solution)/shard_map/bthp,btn->bhpn/dot_general | solution.py:58
  103.9 22.4 %all-gather.4.cloned.1.call-done = f32[128,64,128]{2,1,0:T(8,128)} async-done(((f32[32,64,128]{2,1,0:T(8,128)}), f32[128,64,128]{2,1,0:T(8,128)}) %all-gather.4.cloned.1.call-update) | async-done | bytes 4194320 | tf_op jit(solution)/shard_map/all_gather | solution.py:79
  126.3 3.6 %fusion.15 = (bf16[1,32,64,128]{3,2,1,0:T(8,128)(2,1)S(1)}, bf16[1,32,64,128]{3,2,1,0:T(8,128)(2,1)S(1)}) fusion(f32[128,64,128]{2,1,0:T(8,128)} %all-gather.4.cloned.1.call-done, f32[32]{0:T(128)S(1)} %copy-done.21, f32[32]{0:T(128)S(1)} %copy-done.23, f32[32]{0:T(128)S(1)} %copy-done.24, pred[]{:T(512)S(6)} %lt.46, pred[]{:T(512)S(6)} %lt.45, pred[]{:T(512)S(6)} %lt.44, ...), kind=kLoop, calls=%fused_computation.31 | loop fusion | flops 4718592 | bytes 7340550 | tf_op jit(solution)/shard_map/convert_element_type | solution.py:88
  131.8 1.6 fusion.25
  133.5 32.9 %reduce-scatter.2.cloned.1.call-done = f32[128,288]{0,1:T(8,128)} async-done(((f32[128,2304]{0,1:T(8,128)}), f32[128,288]{0,1:T(8,128)}) %reduce-scatter.2.cloned.1.call-update) | async-done | bytes 147472 | tf_op jit(solution)/shard_map/reduce_scatter | solution.py:119
  166.5 43.2 %all-reduce.2.cloned.1.call-done = f32[128,288]{0,1:T(8,128)} async-done(((f32[128,288]{0,1:T(8,128)}), f32[128,288]{0,1:T(8,128)}) %all-reduce.2.cloned.1.call-update) | async-done | bytes 147472 | tf_op jit(solution)/shard_map/psum | solution.py:120
  209.6 6.6 %collective-permute-done = f32[128,288]{0,1:T(8,128)S(1)} collective-permute-done((f32[128,288]{0,1:T(8,128)}, f32[128,288]{0,1:T(8,128)S(1)}, u32[]{:S(2)}, u32[]{:S(2)}) %collective-permute-start) | collective-permute-done | bytes 147488 | tf_op jit(solution)/shard_map/ppermute | solution.py:129
  216.2 6.4 %collective-permute-done.1 = f32[128,288]{0,1:T(8,128)S(1)} collective-permute-done((f32[128,288]{0,1:T(8,128)S(1)}, f32[128,288]{0,1:T(8,128)S(1)}, u32[]{:S(2)}, u32[]{:S(2)}) %collective-permute-start.1) | collective-permute-done | bytes 147488 | tf_op jit(solution)/shard_map/ppermute | solution.py:129
  222.6 6.4 %collective-permute-done.2 = f32[128,288]{0,1:T(8,128)S(1)} collective-permute-done((f32[128,288]{0,1:T(8,128)S(1)}, f32[128,288]{0,1:T(8,128)S(1)}, u32[]{:S(2)}, u32[]{:S(2)}) %collective-permute-start.2) | collective-permute-done | bytes 147488 | tf_op jit(solution)/shard_map/ppermute | solution.py:129
  228.9 6.4 %collective-permute-done.3 = f32[128,288]{0,1:T(8,128)S(1)} collective-permute-done((f32[128,288]{0,1:T(8,128)S(1)}, f32[128,288]{0,1:T(8,128)S(1)}, u32[]{:S(2)}, u32[]{:S(2)}) %collective-permute-start.3) | collective-permute-done | bytes 147488 | tf_op jit(solution)/shard_map/ppermute | solution.py:129
  235.3 6.4 %collective-permute-done.4 = f32[128,288]{0,1:T(8,128)S(1)} collective-permute-done((f32[128,288]{0,1:T(8,128)S(1)}, f32[128,288]{0,1:T(8,128)S(1)}, u32[]{:S(2)}, u32[]{:S(2)}) %collective-permute-start.4) | collective-permute-done | bytes 147488 | tf_op jit(solution)/shard_map/ppermute | solution.py:129
  241.7 3.3 %convolution_bitcast_fusion.1 = f32[128,32,64]{0,2,1:T(8,128)S(1)} fusion(f32[32,128]{1,0:T(8,128)S(1)} %bitcast.165, f32[32,128]{1,0:T(8,128)S(1)} %bitcast.159, f32[128,128]{0,1:T(8,128)S(1)} %copy-done.15, pred[128,128]{0,1:T(8,128)(4,1)S(1)} %copy-done.19, bf16[4,128,32,64]{1,3,2,0:T(8,128)(2,1)} %bitcast.145, s32[]{:T(128)S(6)} %select_n.96), kind=kOutput, calls=%fused_computation.17 | convolution fusion | flops 70254592 | bytes 1703940 | tf_op jit(solution)/shard_map/hts,shp->thp/dot_general | solution.py:89
  245.0 3.0 %collective-permute-done.5 = f32[128,288]{0,1:T(8,128)S(1)} collective-permute-done((f32[128,288]{0,1:T(8,128)S(1)}, f32[128,288]{0,1:T(8,128)S(1)}, u32[]{:S(2)}, u32[]{:S(2)}) %collective-permute-start.5) | collective-permute-done | bytes 147488 | tf_op jit(solution)/shard_map/ppermute | solution.py:129
  250.1 4.3 %collective-permute-done.6 = f32[128,288]{0,1:T(8,128)S(1)} collective-permute-done((f32[128,288]{0,1:T(8,128)S(1)}, f32[128,288]{0,1:T(8,128)S(1)}, u32[]{:S(2)}, u32[]{:S(2)}) %collective-permute-start.6) | collective-permute-done | bytes 147488 | tf_op jit(solution)/shard_map/ppermute | solution.py:129
  254.9 1.4 copy.66
  (129 shorter events, 20.1 us)
Async XLA Ops:
  7.2 55.4 %copy-start = (bf16[128,2304]{1,0:T(8,128)(2,1)S(1)}, bf16[128,2304]{1,0:T(8,128)(2,1)}, u32[]{:S(2)}) copy-start(bf16[128,2304]{1,0:T(8,128)(2,1)} %param.11) | copy-start | bytes 1769476
  7.2 119.1 %all-gather.4.cloned.1.call-start = ((), (), s32[]{:S(2)}) async-start(), calls=%async_computation.3 | async-start | bytes 5242880 | tf_op jit(solution)/shard_map/all_gather | solution.py:79
  9.8 54.3 %copy-start.25 = (f32[128]{0:T(128)}, f32[128]{0:T(128)S(1)}, u32[]{:S(2)}) copy-start(f32[128]{0:T(128)S(1)} %add_multiply_fusion) | copy-start | bytes 1540
  64.2 13.2 %copy-start.1 = (bf16[512,2304]{1,0:T(8,128)(2,1)}, bf16[512,2304]{1,0:T(8,128)(2,1)S(1)}, u32[]{:S(2)}) copy-start(bf16[512,2304]{1,0:T(8,128)(2,1)S(1)} %convolution_convert_fusion) | copy-start | bytes 7077892
  67.4 11.6 %copy-start.7 = (f32[4,128,32]{2,1,0:T(8,128)}, f32[4,128,32]{2,1,0:T(8,128)S(1)}, u32[]{:S(2)}) copy-start(f32[4,128,32]{2,1,0:T(8,128)S(1)} %reduce_window_sum.35) | copy-start | bytes 196612
  77.1 89.3 %reduce-scatter.2.cloned.1.call-start = ((), (), s32[]{:S(2)}) async-start(), calls=%async_computation.1 | async-start | bytes 1327104 | tf_op jit(solution)/shard_map/reduce_scatter | solution.py:119
  79.6 12.6 %copy-start.6 = (bf16[1,128,2048]{1,2,0:T(8,128)(2,1)S(1)}, bf16[1,128,2048]{1,2,0:T(8,128)(2,1)}, u32[]{:S(2)}) copy-start(bf16[1,128,2048]{1,2,0:T(8,128)(2,1)} %copy.61) | copy-start | bytes 1572868
  82.8 11.7 %copy-start.2 = (bf16[4,128,2048]{1,2,0:T(8,128)(2,1)}, bf16[4,128,2048]{1,2,0:T(8,128)(2,1)S(1)}, u32[]{:S(2)}) copy-start(bf16[4,128,2048]{1,2,0:T(8,128)(2,1)S(1)} %copy.54) | copy-start | bytes 6291460
  89.8 7.4 %copy-start.16 = (f32[1,128,32]{1,0,2:T(1,128)}, f32[1,128,32]{1,0,2:T(1,128)S(1)}, u32[]{:S(2)}) copy-start(f32[1,128,32]{1,0,2:T(1,128)S(1)} %constant_dynamic-slice_fusion.2) | copy-start | bytes 49156
  89.8 7.4 %copy-start.18 = (pred[128,128]{0,1:T(8,128)(4,1)}, pred[128,128]{0,1:T(8,128)(4,1)S(1)}, u32[]{:S(2)}) copy-start(pred[128,128]{0,1:T(8,128)(4,1)S(1)} %iota_compare_fusion) | copy-start | bytes 49156
  90.7 6.4 %copy-start.14 = (f32[128,128]{0,1:T(8,128)}, f32[128,128]{0,1:T(8,128)S(1)}, u32[]{:S(2)}) copy-start(f32[128,128]{0,1:T(8,128)S(1)} %fusion.64) | copy-start | bytes 196612
  92.2 5.0 %copy-start.12 = (f32[1,128,32]{1,2,0:T(8,128)S(1)}, f32[1,128,32]{1,2,0:T(8,128)}, u32[]{:S(2)}) copy-start(f32[1,128,32]{1,2,0:T(8,128)} %copy.57) | copy-start | bytes 49156
  100.3 26.0 %copy-start.21 = (f32[32]{0:T(128)S(1)}, f32[32]{0:T(128)}, u32[]{:S(2)}) copy-start(f32[32]{0:T(128)} %get-tuple-element.14) | copy-start | bytes 388
  100.3 26.0 %copy-start.22 = (f32[32]{0:T(128)S(1)}, f32[32]{0:T(128)}, u32[]{:S(2)}) copy-start(f32[32]{0:T(128)} %get-tuple-element.15) | copy-start | bytes 388
  100.3 26.0 %copy-start.23 = (f32[32]{0:T(128)S(1)}, f32[32]{0:T(128)}, u32[]{:S(2)}) copy-start(f32[32]{0:T(128)} %get-tuple-element.16) | copy-start | bytes 388
  100.3 26.0 %copy-start.24 = (f32[32]{0:T(128)S(1)}, f32[32]{0:T(128)}, u32[]{:S(2)}) copy-start(f32[32]{0:T(128)} %get-tuple-element.17) | copy-start | bytes 388
  126.3 3.7 %copy-start.10 = (f32[128,128]{0,1:T(8,128)S(1)}, f32[128,128]{0,1:T(8,128)}, u32[]{:S(2)}) copy-start(f32[128,128]{0,1:T(8,128)} %fusion.66) | copy-start | bytes 196612
  126.3 4.0 %copy-start.8 = (f32[128,32,64]{0,2,1:T(8,128)S(1)}, f32[128,32,64]{0,2,1:T(8,128)}, u32[]{:S(2)}) copy-start(f32[128,32,64]{0,2,1:T(8,128)} %convolution_bitcast_fusion) | copy-start | bytes 3145732
  126.3 4.0 %copy-start.11 = (f32[1,128,32]{1,2,0:T(8,128)S(1)}, f32[1,128,32]{1,2,0:T(8,128)}, u32[]{:S(2)}) copy-start(f32[1,128,32]{1,2,0:T(8,128)} %copy.64) | copy-start | bytes 49156
  131.4 110.3 %copy-start.13 = (f32[1,128,32]{1,2,0:T(8,128)S(1)}, f32[1,128,32]{1,2,0:T(8,128)}, u32[]{:S(2)}) copy-start(f32[1,128,32]{1,2,0:T(8,128)} %copy.57) | copy-start | bytes 49156
  131.4 110.3 %copy-start.15 = (f32[128,128]{0,1:T(8,128)S(1)}, f32[128,128]{0,1:T(8,128)}, u32[]{:S(2)}) copy-start(f32[128,128]{0,1:T(8,128)} %copy-done.14) | copy-start | bytes 196612
  131.4 110.2 %copy-start.17 = (f32[1,128,32]{1,0,2:T(1,128)S(1)}, f32[1,128,32]{1,0,2:T(1,128)}, u32[]{:S(2)}) copy-start(f32[1,128,32]{1,0,2:T(1,128)} %copy-done.16) | copy-start | bytes 49156
  131.4 110.2 %copy-start.19 = (pred[128,128]{0,1:T(8,128)(4,1)S(1)}, pred[128,128]{0,1:T(8,128)(4,1)}, u32[]{:S(2)}) copy-start(pred[128,128]{0,1:T(8,128)(4,1)} %copy-done.18) | copy-start | bytes 49156
  133.4 76.2 %all-reduce.2.cloned.1.call-start = ((), (), s32[]{:S(2)}) async-start(), calls=%async_computation.2 | async-start | bytes 294912 | tf_op jit(solution)/shard_map/psum | solution.py:120
  209.6 6.6 %collective-permute-start = (f32[128,288]{0,1:T(8,128)}, f32[128,288]{0,1:T(8,128)S(1)}, u32[]{:S(2)}, u32[]{:S(2)}) collective-permute-start(f32[128,288]{0,1:T(8,128)} %all-reduce.2.cloned.1.call-done), channel_id=1, source_target_pairs={{0,1},{1,2},{2,3},{3,4},{4,5},{5,6},{6,7},{7,0},{8,9},{9,10},{10,1... | collective-permute-start | bytes 442376 | tf_op jit(solution)/shard_map/ppermute | solution.py:129
  216.2 6.4 %collective-permute-start.1 = (f32[128,288]{0,1:T(8,128)S(1)}, f32[128,288]{0,1:T(8,128)S(1)}, u32[]{:S(2)}, u32[]{:S(2)}) collective-permute-start(f32[128,288]{0,1:T(8,128)S(1)} %collective-permute-done), channel_id=1, source_target_pairs={{0,1},{1,2},{2,3},{3,4},{4,5},{5,6},{6,7},{7,0},{8,9},{9,10},{10,1... | collective-permute-start | bytes 442376 | tf_op jit(solution)/shard_map/ppermute | solution.py:129
  222.6 6.4 %collective-permute-start.2 = (f32[128,288]{0,1:T(8,128)S(1)}, f32[128,288]{0,1:T(8,128)S(1)}, u32[]{:S(2)}, u32[]{:S(2)}) collective-permute-start(f32[128,288]{0,1:T(8,128)S(1)} %collective-permute-done.1), channel_id=1, source_target_pairs={{0,1},{1,2},{2,3},{3,4},{4,5},{5,6},{6,7},{7,0},{8,9},{9,10},{10,1... | collective-permute-start | bytes 442376 | tf_op jit(solution)/shard_map/ppermute | solution.py:129
  228.9 6.4 %collective-permute-start.3 = (f32[128,288]{0,1:T(8,128)S(1)}, f32[128,288]{0,1:T(8,128)S(1)}, u32[]{:S(2)}, u32[]{:S(2)}) collective-permute-start(f32[128,288]{0,1:T(8,128)S(1)} %collective-permute-done.2), channel_id=1, source_target_pairs={{0,1},{1,2},{2,3},{3,4},{4,5},{5,6},{6,7},{7,0},{8,9},{9,10},{10,1... | collective-permute-start | bytes 442376 | tf_op jit(solution)/shard_map/ppermute | solution.py:129
  235.3 6.4 %collective-permute-start.4 = (f32[128,288]{0,1:T(8,128)S(1)}, f32[128,288]{0,1:T(8,128)S(1)}, u32[]{:S(2)}, u32[]{:S(2)}) collective-permute-start(f32[128,288]{0,1:T(8,128)S(1)} %collective-permute-done.3), channel_id=1, source_target_pairs={{0,1},{1,2},{2,3},{3,4},{4,5},{5,6},{6,7},{7,0},{8,9},{9,10},{10,1... | collective-permute-start | bytes 442376 | tf_op jit(solution)/shard_map/ppermute | solution.py:129
  241.7 6.4 %collective-permute-start.5 = (f32[128,288]{0,1:T(8,128)S(1)}, f32[128,288]{0,1:T(8,128)S(1)}, u32[]{:S(2)}, u32[]{:S(2)}) collective-permute-start(f32[128,288]{0,1:T(8,128)S(1)} %collective-permute-done.4), channel_id=1, source_target_pairs={{0,1},{1,2},{2,3},{3,4},{4,5},{5,6},{6,7},{7,0},{8,9},{9,10},{10,1... | collective-permute-start | bytes 442376 | tf_op jit(solution)/shard_map/ppermute | solution.py:129
  245.0 9.6 %copy-start.9 = (f32[128,288]{0,1:T(8,128)S(1)}, f32[128,288]{0,1:T(8,128)}, u32[]{:S(2)}) copy-start(f32[128,288]{0,1:T(8,128)} %all-reduce.2.cloned.1.call-done) | copy-start | bytes 442372
  248.0 6.4 %collective-permute-start.6 = (f32[128,288]{0,1:T(8,128)S(1)}, f32[128,288]{0,1:T(8,128)S(1)}, u32[]{:S(2)}, u32[]{:S(2)}) collective-permute-start(f32[128,288]{0,1:T(8,128)S(1)} %collective-permute-done.5), channel_id=1, source_target_pairs={{0,1},{1,2},{2,3},{3,4},{4,5},{5,6},{6,7},{7,0},{8,9},{9,10},{10,1... | collective-permute-start | bytes 442376 | tf_op jit(solution)/shard_map/ppermute | solution.py:129
  (9 other events, 17.7 us)
Sparse Core Ops, SparseCore 0:
  77.2 48.9 all-gather.3
  133.6 32.8 reduce-scatter.1
  169.3 40.2 all-reduce.1
